TPU v7x, 256 devices: a whole 4x4x8 slice. The times are simulated.
256 devices in a mesh: expert: 8 (over x, core), tensor: 32 (over z, y).
Axes of the slice: x: 4, y: 4, z: 8, core: 2. Of those that a mesh axis runs over, the one named last changes fastest.
Arguments:
- resid: bfloat16 [16384, 2048], P(('expert', 'tensor')), may hold values from -6 to 6
- contexts: bfloat16 [16384, 4096], P('expert', 'tensor'), may hold values from -6 to 6
- att_routes: int32 [16384, 2], P('expert'), may hold values from 0 to 7, all different within a row
- att_scores: float32 [16384, 2], P('expert'), may hold values from -6 to 6
- att_out_w: bfloat16 [8, 2048, 2048], P(None, 'tensor'), may hold values from -0.125 to 0.125
- norm_gain: bfloat16 [2048], replicated, may hold values from 0.25 to 1.75
- router_w: bfloat16 [2048, 8], replicated, may hold values from -0.125 to 0.125
- mlp_routes: int32 [16384, 2], P(('expert', 'tensor')), may hold values from 0 to 7, all different within a row
- split_rule: int32 [16384, 2], P(('expert', 'tensor')), may hold values from 0 to 2519
- placement: int32 [32], replicated, may hold values from 0 to 7, as said below
- cap_blocks: int32 [32], replicated, may hold values from 1 to 2, as said below
- w_gate_up: bfloat16 [32, 2048, 2, 5632], P('tensor', None, None, 'expert'), as said below
- w_down: bfloat16 [32, 5632, 2048], P('tensor', 'expert'), as said below
- final_gain: bfloat16 [2048], replicated, may hold values from 0.25 to 1.75
Outputs:
- stream_out: bfloat16 [16384, 2048], P(('expert', 'tensor'))
- normalized: bfloat16 [16384, 2048], P(('expert', 'tensor'))
Inputs may be any that keep to these rules, and one draw needn't show every extreme that they name: `att_routes`: each row names 2 different experts. `mlp_routes`: each row names 2 different experts. `placement`: every expert is held by at least one slot. `cap_blocks`: some slot accepts 2 blocks. `w_gate_up`: slots that hold the same expert hold equal weights. `w_down`: slots that hold the same expert hold equal weights.
All inputs are finite; a program needn't handle non-finite values.
Results may differ from a plain program's by a relative error of at most 0.023.
Values may be sent and summed in bfloat16 or wider, within the bound.
No kernel may reach another device: no remote copies, remote signals or barrier semaphores. Data moves between devices by JAX's collectives and lax.ppermute only.
A program may use at most 64 MiB of HBM per device.

v0:
```python
import jax
import jax.numpy as jnp
from jax import lax
from jax.sharding import Mesh, PartitionSpec as P

MAXB = 2
TENSOR = ("tz", "ty")
norm_eps = 1e-06


def rms_norm(values, gain):
    scale = lax.rsqrt(jnp.mean(values * values, axis=-1, keepdims=True) + norm_eps)
    return values * scale * gain.astype(values.dtype)


def pair_gates(scores):
    first = jax.nn.silu(scores[:, 0:1] * 0.0) * 0.0 + jax.nn.sigmoid(
        scores[:, 0:1] - scores[:, 1:2]
    )
    first = first[:, 0]
    return jnp.stack([first, 1.0 - first], axis=1)


def activate(shard_piece, w_gate_up):
    both = jnp.einsum(
        "tsecd,sdgf->tsecgf", shard_piece, w_gate_up, preferred_element_type=jnp.float32
    )
    hidden = (jax.nn.silu(both[:, :, :, :, 0, :]) * both[:, :, :, :, 1, :]).astype(jnp.bfloat16)
    hidden = jnp.transpose(hidden, (0, 2, 3, 1, 4))
    return hidden.reshape(
        hidden.shape[0] * hidden.shape[1] * hidden.shape[2], hidden.shape[3], hidden.shape[4]
    )


def per_device(
    resid,
    contexts,
    att_routes,
    att_scores,
    att_out_w,
    norm_gain,
    router_w,
    mlp_routes,
    split_rule,
    placement,
    cap_blocks,
    w_gate_up,
    w_down,
    final_gain,
):
    n_tensor = lax.axis_size(TENSOR)
    row_count = resid.shape[0]
    model_width = resid.shape[1]
    group_rows = contexts.shape[0]
    att_experts = att_out_w.shape[0]
    slice_ctx = att_out_w.shape[1]
    top_count = att_routes.shape[1]
    gate_att = pair_gates(att_scores)
    chosen = (
        att_routes[:, :, None] == jnp.arange(att_experts, dtype=jnp.int32)[None, None, :]
    ).astype(jnp.float32)
    weighted = chosen * gate_att[:, :, None]
    context_part = contexts.reshape(group_rows, slice_ctx, top_count).astype(jnp.float32)
    mixed = (
        jnp.einsum("tke,tck->tec", weighted, context_part)
        .astype(jnp.bfloat16)
        .reshape(group_rows, att_experts * slice_ctx)
    )
    weight_flat = att_out_w.reshape(att_experts * slice_ctx, model_width)
    row_block = mixed
    partial = jnp.dot(row_block, weight_flat, preferred_element_type=jnp.float32).astype(
        jnp.bfloat16
    )
    partial = lax.psum_scatter(partial, "tz", scatter_dimension=0, tiled=True)
    attention = lax.psum_scatter(partial, "ty", scatter_dimension=0, tiled=True).astype(jnp.float32)
    stream = (resid.astype(jnp.float32) + attention).astype(jnp.bfloat16)
    normed = rms_norm(stream.astype(jnp.float32), norm_gain).astype(jnp.bfloat16)
    logits = jnp.dot(normed, router_w, preferred_element_type=jnp.float32)
    gate_mlp = pair_gates(jnp.take_along_axis(logits, mlp_routes, axis=1))
    replicas = placement.shape[0]
    slots = w_gate_up.shape[0]
    expert_total = router_w.shape[1]
    block_rows = max(1, row_count * top_count // (2 * replicas))
    capacity_rows = MAXB * block_rows
    slot_ids = jnp.arange(replicas, dtype=jnp.int32)
    expert_ids = jnp.arange(expert_total, dtype=jnp.int32)
    copies = jnp.sum((placement[None, :] == expert_ids[:, None]).astype(jnp.int32), axis=1)
    earlier = jnp.sum(
        (
            (placement[None, :] == placement[:, None]) & (slot_ids[None, :] < slot_ids[:, None])
        ).astype(jnp.int32),
        axis=1,
    )
    route_onehot = (mlp_routes[:, :, None] == expert_ids[None, None, :]).astype(jnp.int32)
    route_copies = jnp.sum(route_onehot * copies[None, None, :], axis=2)
    replica_rank = jnp.remainder(split_rule, route_copies)
    match = (
        (placement[None, None, :] == mlp_routes[:, :, None])
        & (earlier[None, None, :] == replica_rank[:, :, None])
    ).astype(jnp.int32)
    replica_slot = jnp.sum(match * slot_ids[None, None, :], axis=2)
    capacity = jnp.sum(match * cap_blocks[None, None, :], axis=2) * block_rows
    flat_match = match.reshape(row_count * top_count, replicas)
    before = jnp.cumsum(flat_match, axis=0) - flat_match
    arrival = jnp.sum(before * flat_match, axis=1).reshape(row_count, top_count)
    is_kept = arrival < capacity
    holder = replica_slot // slots
    within = replica_slot % slots
    position = within * (n_tensor * capacity_rows) + holder * capacity_rows + arrival
    position = jnp.where(is_kept, position, -1)
    buffer_rows = slots * n_tensor * capacity_rows
    placer = jnp.sum(
        (jnp.arange(buffer_rows, dtype=jnp.int32)[:, None, None] == position[None, :, :]).astype(
            jnp.bfloat16
        ),
        axis=2,
    )
    send_rows = jnp.dot(placer, normed, preferred_element_type=jnp.float32).astype(jnp.bfloat16)
    send_rows = send_rows.reshape(slots, n_tensor, capacity_rows, model_width)
    exchanged = lax.all_to_all(send_rows, TENSOR, split_axis=1, concat_axis=1, tiled=True)
    arrived = lax.all_gather(exchanged[None], "expert", axis=0, tiled=True)
    hidden = activate(arrived, w_gate_up)
    row_block = hidden
    summed = lax.psum_scatter(
        jnp.einsum("bsf,sfd->bsd", row_block, w_down, preferred_element_type=jnp.float32).astype(
            jnp.bfloat16
        ),
        "expert",
        scatter_dimension=0,
        tiled=True,
    )
    results = summed.reshape(n_tensor, capacity_rows, slots, model_width)
    returned = lax.all_to_all(results, TENSOR, split_axis=0, concat_axis=0, tiled=True)
    flat_back = returned.reshape(n_tensor * capacity_rows * slots, model_width)
    back_index = jnp.where(is_kept, holder * (capacity_rows * slots) + arrival * slots + within, 0)
    fetched = (
        jnp.take(flat_back, back_index.reshape(-1), axis=0)
        .reshape(row_count, top_count, model_width)
        .astype(jnp.float32)
    )
    factors = gate_mlp * is_kept.astype(jnp.float32)
    expert_mix = fetched[:, 0, :] * factors[:, 0:1] + fetched[:, 1, :] * factors[:, 1:2]
    after = stream.astype(jnp.float32) + expert_mix
    return (after.astype(jnp.bfloat16), rms_norm(after, final_gain).astype(jnp.bfloat16))


def split_mesh(mesh):
    n_expert, n_tensor = mesh.devices.shape
    n_y = 4 if n_tensor % 4 == 0 else 1
    return Mesh(mesh.devices.reshape(n_expert, n_tensor // n_y, n_y), ("expert", "tz", "ty"))


def solution(mesh):
    mesh = split_mesh(mesh)
    return jax.shard_map(
        per_device,
        mesh=mesh,
        in_specs=(
            P(("expert", "tz", "ty"), None),
            P("expert", TENSOR),
            P("expert", None),
            P("expert", None),
            P(None, TENSOR, None),
            P(),
            P(),
            P(("expert", "tz", "ty"), None),
            P(("expert", "tz", "ty"), None),
            P(),
            P(),
            P(TENSOR, None, None, "expert"),
            P(TENSOR, "expert", None),
            P(),
        ),
        out_specs=(P(("expert", "tz", "ty"), None), P(("expert", "tz", "ty"), None)),
        check_vma=False,
    )
```

profile of v0, /device:TPU:7, one launch (start us, length us, event | category | flops | bytes accessed | tf_op | source)
XLA Modules:
  0.0 327.3 jit_solution(1362483452195812732)
XLA Ops:
  7.2 0.0 reduce-scatter.4.cloned.1.call-start
  7.2 2.2 copy.76
  9.4 1.4 reshape.178
  10.8 2.1 copy.77
  12.9 0.1 broadcast_subtract_fusion
  13.0 0.3 copy.75
  13.3 1.4 copy.74
  14.7 14.3 %convolution_convert_fusion = bf16[2048,8,64]{2,1,0:T(8,128)(2,1)S(1)} fusion(bf16[2048,64,2]{1,2,0:T(2,128)(2,1)} %copy.77, bf16[2048,2]{1,0:T(8,128)(2,1)S(1)} %copy.75, s32[2048,2]{1,0:T(8,128)} %copy.74), kind=kOutput, calls=%fused_computation.13 | convolution fusion | flops 4259840 | bytes 2646016 | tf_op jit(solution)/shard_map/tke,tck->tec/dot_general | solution.py:65
  29.0 7.0 %bitcast_convert_fusion = bf16[2048,2048]{1,0:T(8,128)(2,1)} fusion(bf16[8,64,2048]{2,1,0:T(8,128)(2,1)S(1)} %copy-done.11, bf16[2048,8,64]{2,1,0:T(8,128)(2,1)S(1)} %convolution_convert_fusion), kind=kOutput, calls=%fused_computation.2 | convolution fusion | flops 4299161600 | bytes 12582912 | tf_op jit(solution)/shard_map/dot_general | solution.py:71
  36.0 0.0 reduce-scatter.4.cloned.1.call-update
  36.0 0.0 reduce-scatter.6.cloned.1.call-start
  36.1 98.0 %reduce-scatter.4.cloned.1.call-done = bf16[256,2048]{1,0:T(8,128)(2,1)} async-done(((bf16[2048,2048]{1,0:T(8,128)(2,1)}), bf16[256,2048]{1,0:T(8,128)(2,1)}) %reduce-scatter.4.cloned.1.call-update) | async-done | bytes 1048592 | tf_op jit(solution)/shard_map/reduce_scatter | solution.py:74
  134.0 0.0 reduce-scatter.6.cloned.1.call-update
  134.1 0.0 all-gather.3.cloned.1.call-start
  134.1 0.1 copy.79
  134.2 0.1 convert_reduce_fusion.1
  134.4 0.1 select_reduce_fusion.3
  134.5 0.1 and_select_fusion.1
  134.6 0.1 copy.80
  134.7 0.1 eq.133
  134.8 0.1 eq.119
  135.0 0.2 convert_reduce_fusion
  135.1 0.1 fusion.26
  135.3 0.2 reduce_window_sum.11
  135.4 0.2 select_reduce_fusion
  135.6 0.1 reduce_sum.92
  135.8 0.1 copy.81
  135.8 0.1 select_reduce_fusion.2
  136.0 0.1 fusion.27
  136.0 23.9 %reduce-scatter.6.cloned.1.call-done = bf16[64,2048]{1,0:T(8,128)(2,1)} async-done(((bf16[256,2048]{1,0:T(8,128)(2,1)}), bf16[64,2048]{1,0:T(8,128)(2,1)}) %reduce-scatter.6.cloned.1.call-update) | async-done | bytes 262160 | tf_op jit(solution)/shard_map/reduce_scatter | solution.py:75
  160.0 1.1 fusion.15
  161.1 1.1 convolution_convert_fusion.1
  162.3 2.0 reshape.179
  164.3 21.4 %all_to_all.10 = bf16[1,32,4,2048]{3,2,0,1:T(4,128)(2,1)S(1)} all-to-all(bf16[1,32,4,2048]{3,2,0,1:T(4,128)(2,1)} %bitcast.82), channel_id=1, replica_groups=mesh['expert'=8,'tz'=8,'ty'=4] {'tz','ty'}, dimensions={1} | all-to-all | bytes 1048576 | tf_op jit(solution)/shard_map/all_to_all | solution.py:120
  185.7 1.1 copy.84
  186.8 0.0 all-gather.3.cloned.1.call-update
  186.8 0.2 reduce-scatter.8.cloned.1.call-start
  187.0 33.9 %all-gather.3.cloned.1.call-done = bf16[8,32,4,2048]{3,1,2,0:T(8,128)(2,1)} async-done(((bf16[1,32,4,2048]{3,1,2,0:T(8,128)(2,1)}), bf16[8,32,4,2048]{3,1,2,0:T(8,128)(2,1)}) %all-gather.3.cloned.1.call-update) | async-done | bytes 4194320 | tf_op jit(solution)/shard_map/all_gather | solution.py:121
  220.9 10.0 %fusion.6 = f32[8,1,32,4,2,704]{5,2,4,3,0,1:T(8,128)S(1)} fusion(bf16[1,2048,2,704]{1,3,2,0:T(8,128)(2,1)} %param.25, bf16[8,32,4,2048]{3,1,2,0:T(8,128)(2,1)} %all-gather.3.cloned.1.call-done), kind=kOutput, calls=%fused_computation.12 | convolution fusion | flops 5905580032 | bytes 15728640 | tf_op jit(solution)/shard_map/tsecd,sdgf->tsecgf/dot_general | solution.py:25
  230.9 1.0 fusion.4
  231.9 2.4 copy.85
  234.3 3.7 %convert_element_type.95 = bf16[1024,704]{1,0:T(8,128)(2,1)} reshape(bf16[8,1,32,4,1,704]{5,3,2,0,4,1:T(4,128)(2,1)} %copy.85) | data formatting | bytes 2883584 | tf_op jit(solution)/shard_map/convert_element_type | solution.py:28
  238.1 6.4 %convert_bitcast_fusion = bf16[1024,1,2048]{2,0,1:T(8,128)(2,1)} fusion(bf16[1024,704]{1,0:T(8,128)(2,1)} %convert_element_type.95, bf16[1,704,2048]{2,1,0:T(8,128)(2,1)S(1)} %copy-done), kind=kOutput, calls=%fused_computation.7 | convolution fusion | flops 2954887168 | bytes 8519680 | tf_op jit(solution)/shard_map/bsf,sfd->bsd/dot_general | solution.py:125
  244.4 0.0 reduce-scatter.8.cloned.1.call-update
  244.5 0.1 copy.90
  244.6 0.1 reshape.194
  244.7 0.1 copy.88
  244.8 0.1 mul.206
  244.9 0.1 copy.87
  245.0 0.1 mul.205
  245.2 39.8 %reduce-scatter.8.cloned.1.call-done = bf16[128,1,2048]{2,0,1:T(8,128)(2,1)} async-done(((bf16[1024,1,2048]{2,0,1:T(8,128)(2,1)}), bf16[128,1,2048]{2,0,1:T(8,128)(2,1)}) %reduce-scatter.8.cloned.1.call-update) | async-done | bytes 524304 | tf_op jit(solution)/shard_map/reduce_scatter | solution.py:124
  285.0 2.0 reshape.183
  287.1 9.7 %all-to-all-start.1 = ((bf16[32,4,1,2048]{3,1,2,0:T(4,128)(2,1)}), bf16[32,4,1,2048]{3,1,2,0:T(4,128)(2,1)}, u32[]{:S(2)}, u32[]{:S(2)}) async-start(bf16[32,4,1,2048]{3,1,2,0:T(4,128)(2,1)} %bitcast.81), calls=%async_computation.4 | async-start | bytes 1048576 | tf_op jit(solution)/shard_map/all_to_all | solution.py:133
  296.8 0.2 fusion.22
  297.0 1.0 gather_fusion.1
  298.1 0.1 reshape.197
  298.2 0.1 copy.91
  298.3 15.7 %all-to-all-done.1 = bf16[32,4,1,2048]{3,1,2,0:T(4,128)(2,1)} async-done(((bf16[32,4,1,2048]{3,1,2,0:T(4,128)(2,1)}), bf16[32,4,1,2048]{3,1,2,0:T(4,128)(2,1)}, u32[]{:S(2)}, u32[]{:S(2)}) %all-to-all-start.1) | async-done | bytes 524320 | tf_op jit(solution)/shard_map/all_to_all | solution.py:133
  314.1 1.2 reshape.184
  315.2 1.7 gather_fusion
  317.0 1.4 gather.11
  318.3 0.3 fusion.21
  318.7 1.2 multiply_reduce_fusion
  320.0 0.8 multiply_convert_fusion
  (40 shorter events, 0.2 us)
Async XLA Ops:
  7.2 230.9 %copy-start = (bf16[1,704,2048]{2,1,0:T(8,128)(2,1)S(1)}, bf16[1,704,2048]{2,1,0:T(8,128)(2,1)}, u32[]{:S(2)}) copy-start(bf16[1,704,2048]{2,1,0:T(8,128)(2,1)} %param.26) | copy-start | bytes 8650756
  7.2 5.7 %copy-start.5 = (f32[2048,2]{0,1:T(2,128)S(1)}, f32[2048,2]{0,1:T(2,128)}, u32[]{:S(2)}) copy-start(f32[2048,2]{0,1:T(2,128)} %param.17) | copy-start | bytes 49156
  7.2 6.1 %copy-start.4 = (s32[2048,2]{0,1:T(2,128)S(1)}, s32[2048,2]{0,1:T(2,128)}, u32[]{:S(2)}) copy-start(s32[2048,2]{0,1:T(2,128)} %param.16) | copy-start | bytes 49156
  7.2 126.8 %reduce-scatter.4.cloned.1.call-start = ((), (), s32[]{:S(2)}) async-start(), calls=%async_computation.5 | async-start | bytes 9437184 | tf_op jit(solution)/shard_map/reduce_scatter | solution.py:74
  14.7 14.3 %copy-start.11 = (bf16[8,64,2048]{2,1,0:T(8,128)(2,1)S(1)}, bf16[8,64,2048]{2,1,0:T(8,128)(2,1)}, u32[]{:S(2)}) copy-start(bf16[8,64,2048]{2,1,0:T(8,128)(2,1)} %param.18) | copy-start | bytes 6291460
  36.0 98.2 %copy-start.7 = (bf16[2048]{0:T(1024)(128)(2,1)S(1)}, bf16[2048]{0:T(1024)(128)(2,1)}, u32[]{:S(2)}) copy-start(bf16[2048]{0:T(1024)(128)(2,1)} %param.19) | copy-start | bytes 12292
  36.0 98.2 %copy-start.3 = (s32[64,2]{0,1:T(2,128)S(1)}, s32[64,2]{0,1:T(2,128)}, u32[]{:S(2)}) copy-start(s32[64,2]{0,1:T(2,128)} %param.21) | copy-start | bytes 1540
  36.0 98.3 %copy-start.6 = (s32[32]{0:T(128)S(1)}, s32[32]{0:T(128)}, u32[]{:S(2)}) copy-start(s32[32]{0:T(128)} %param.23) | copy-start | bytes 388
  36.0 98.5 %copy-start.9 = (s32[64,2]{0,1:T(2,128)S(1)}, s32[64,2]{0,1:T(2,128)}, u32[]{:S(2)}) copy-start(s32[64,2]{0,1:T(2,128)} %param.22) | copy-start | bytes 1540
  36.0 99.9 %copy-start.10 = (s32[32]{0:T(128)S(1)}, s32[32]{0:T(128)}, u32[]{:S(2)}) copy-start(s32[32]{0:T(128)} %param.24) | copy-start | bytes 388
  36.0 124.0 %copy-start.2 = (bf16[64,2048]{1,0:T(8,128)(2,1)S(1)}, bf16[64,2048]{1,0:T(8,128)(2,1)}, u32[]{:S(2)}) copy-start(bf16[64,2048]{1,0:T(8,128)(2,1)} %param.14) | copy-start | bytes 786436
  36.0 123.9 %reduce-scatter.6.cloned.1.call-start = ((), (), s32[]{:S(2)}) async-start(), calls=%async_computation.6 | async-start | bytes 1310720 | tf_op jit(solution)/shard_map/reduce_scatter | solution.py:75
  134.1 86.9 %all-gather.3.cloned.1.call-start = ((), (), s32[]{:S(2)}) async-start(), calls=%async_computation.8 | async-start | bytes 4718592 | tf_op jit(solution)/shard_map/all_gather | solution.py:121
  161.1 135.7 %copy-start.1 = (bf16[64,2048]{1,0:T(8,128)(2,1)}, bf16[64,2048]{1,0:T(8,128)(2,1)S(1)}, u32[]{:S(2)}) copy-start(bf16[64,2048]{1,0:T(8,128)(2,1)S(1)} %get-tuple-element.9) | copy-start | bytes 786436
  186.8 98.2 %reduce-scatter.8.cloned.1.call-start = ((), (), s32[]{:S(2)}) async-start(), calls=%async_computation.7 | async-start | bytes 4718592 | tf_op jit(solution)/shard_map/reduce_scatter | solution.py:124
  244.4 0.8 copy-start.8
  244.4 52.4 %copy-start.12 = (bf16[2048,8]{0,1:T(8,128)(2,1)S(1)}, bf16[2048,8]{0,1:T(8,128)(2,1)}, u32[]{:S(2)}) copy-start(bf16[2048,8]{0,1:T(8,128)(2,1)} %param.20) | copy-start | bytes 98308
  287.1 27.0 %all-to-all-start.1 = ((bf16[32,4,1,2048]{3,1,2,0:T(4,128)(2,1)}), bf16[32,4,1,2048]{3,1,2,0:T(4,128)(2,1)}, u32[]{:S(2)}, u32[]{:S(2)}) async-start(bf16[32,4,1,2048]{3,1,2,0:T(4,128)(2,1)} %bitcast.81), calls=%async_computation.4 | async-start | bytes 1048576 | tf_op jit(solution)/shard_map/all_to_all | solution.py:133
Sparse Core Ops, SparseCore 0:
  36.1 97.8 reduce-scatter.3
  136.6 23.3 reduce-scatter.5
  186.9 33.9 all-gather.2
  244.6 40.4 reduce-scatter.7
where the time goes:
time: 328 us; the launch traced here: 327 us
  waiting for transfers between devices  211 us (64%)
  matrix products  39 us (12%)
  local copies, waits for them, and re-layouts  25.6 us (8%)
  blocking collectives  21.4 us (7%)
  between operations  14.1 us (4%)
  starting transfers between devices  10 us (3%)
  other arithmetic  5.93 us (2%)
    reduce_scatter x1, waiting for transfers between devices, per_device(): partial = lax.psum_scatter(partial, 'tz', scatter_dimension=0, tiled=True)  98 us
    reduce_scatter x1, waiting for transfers between devices, per_device(): lax.psum_scatter(jnp.einsum('bsf,sfd->bsd', row_block, w_down, preferred_...  39.8 us
    all_gather x1, waiting for transfers between devices, per_device(): arrived = lax.all_gather(exchanged[None], 'expert', axis=0, tiled=True)  33.9 us
    reduce_scatter x1, waiting for transfers between devices, per_device(): lax.psum_scatter(partial, 'ty', scatter_dimension=0, tiled=True)  23.9 us
    all_to_all x1, blocking collectives, per_device(): lax.all_to_all(send_rows, TENSOR, split_axis=1, concat_axis=1, tiled=True)  21.4 us
    all_to_all x1, waiting for transfers between devices, per_device(): lax.all_to_all(results, TENSOR, split_axis=0, concat_axis=0, tiled=True)  15.7 us
    dot_general x1, matrix products, per_device(): jnp.einsum('tke,tck->tec', weighted, context_part).astype(jnp.bfloat16)  14.3 us
    dot_general x1, matrix products, activate(): jnp.einsum('tsecd,sdgf->tsecgf', shard_piece, w_gate_up, preferred_elemen...  9.98 us
  transfers between devices with their start and end apart: 5, of which 5 were waited for; matrix products, arithmetic and copies ran while one was open for 1% of the time, Pallas kernels for 0%

commit v1 on v0

--- a/solution.py
+++ b/solution.py
@@ -118,7 +118,11 @@
     send_rows = jnp.dot(placer, normed, preferred_element_type=jnp.float32).astype(jnp.bfloat16)
     send_rows = send_rows.reshape(slots, n_tensor, capacity_rows, model_width)
     exchanged = lax.all_to_all(send_rows, TENSOR, split_axis=1, concat_axis=1, tiled=True)
-    arrived = lax.all_gather(exchanged[None], "expert", axis=0, tiled=True)
+    size = lax.axis_size("expert")
+    repeats = [size if d == 0 else 1 for d in range(exchanged[None].ndim)]
+    arrived = lax.all_to_all(
+        jnp.tile(exchanged[None], repeats), "expert", split_axis=0, concat_axis=0, tiled=True
+    )
     hidden = activate(arrived, w_gate_up)
     row_block = hidden
     summed = lax.psum_scatter(

time: 328 us -> 342 us (1.043)
  blocking collectives: 21.4 us -> 78.9 us
  waiting for transfers between devices: 211 us -> 172 us
    all_to_all x0 -> x1, blocking collectives: none -> 57.6 us  [per_device(): lax.all_to_all(jnp.tile(exchanged[None], repeats), 'expert', split_axis=0...]
    all_gather x1 -> x0, waiting for transfers between devices: 33.9 us -> none  [per_device(): arrived = lax.all_gather(exchanged[None], 'expert', axis=0, tiled=True)]
    reduce_scatter x1, waiting for transfers between devices: 39.8 us -> 34.3 us  [per_device(): lax.psum_scatter(jnp.einsum('bsf,sfd->bsd', row_block, w_down, preferred_...]
  transfers between devices with their start and end apart: 5 -> 4, of which waited for: 5 -> 4; matrix products, arithmetic and copies ran while one was open for 1% -> 1% of each run, Pallas kernels for 0% -> 0%
where the time goes in v1:
time: 342 us
  waiting for transfers between devices  172 us (50%)
  blocking collectives  78.9 us (23%)
  matrix products  35.7 us (10%)
  local copies, waits for them, and re-layouts  25.3 us (7%)
  between operations  14.1 us (4%)
  starting transfers between devices  9.86 us (3%)
  other arithmetic  5.93 us (2%)
    reduce_scatter x1, waiting for transfers between devices, per_device(): partial = lax.psum_scatter(partial, 'tz', scatter_dimension=0, tiled=True)  98 us
    all_to_all x1, blocking collectives, per_device(): lax.all_to_all(jnp.tile(exchanged[None], repeats), 'expert', split_axis=0...  57.6 us
    reduce_scatter x1, waiting for transfers between devices, per_device(): lax.psum_scatter(jnp.einsum('bsf,sfd->bsd', row_block, w_down, preferred_...  34.3 us
    reduce_scatter x1, waiting for transfers between devices, per_device(): lax.psum_scatter(partial, 'ty', scatter_dimension=0, tiled=True)  23.9 us
    all_to_all x1, blocking collectives, per_device(): lax.all_to_all(send_rows, TENSOR, split_axis=1, concat_axis=1, tiled=True)  21.4 us
    all_to_all x1, waiting for transfers between devices, per_device(): lax.all_to_all(results, TENSOR, split_axis=0, concat_axis=0, tiled=True)  15.7 us
    dot_general x1, matrix products, per_device(): jnp.einsum('tke,tck->tec', weighted, context_part).astype(jnp.bfloat16)  14.3 us
    all_to_all x1, starting transfers between devices, per_device(): lax.all_to_all(results, TENSOR, split_axis=0, concat_axis=0, tiled=True)  9.74 us
  transfers between devices with their start and end apart: 4, of which 4 were waited for; matrix products, arithmetic and copies ran while one was open for 1% of the time, Pallas kernels for 0%

profile of v1, /device:TPU:7, one launch (start us, length us, event | category | flops | bytes accessed | tf_op | source)
XLA Modules:
  0.0 341.8 jit_solution(15637602632583291146)
XLA Ops:
  7.2 0.0 copy-start
  7.2 0.0 reduce-scatter.4.cloned.1.call-start
  7.2 2.2 copy.76
  9.4 1.4 reshape.181
  10.8 2.1 copy.77
  12.9 0.1 broadcast_subtract_fusion
  13.0 0.3 copy.75
  13.3 1.4 copy.74
  14.7 14.3 %convolution_convert_fusion = bf16[2048,8,64]{2,1,0:T(8,128)(2,1)S(1)} fusion(bf16[2048,64,2]{1,2,0:T(2,128)(2,1)} %copy.77, bf16[2048,2]{1,0:T(8,128)(2,1)S(1)} %copy.75, s32[2048,2]{1,0:T(8,128)} %copy.74), kind=kOutput, calls=%fused_computation.13 | convolution fusion | flops 4259840 | bytes 2646016 | tf_op jit(solution)/shard_map/tke,tck->tec/dot_general | solution.py:65
  29.0 7.0 %bitcast_convert_fusion = bf16[2048,2048]{1,0:T(8,128)(2,1)} fusion(bf16[8,64,2048]{2,1,0:T(8,128)(2,1)S(1)} %copy-done.11, bf16[2048,8,64]{2,1,0:T(8,128)(2,1)S(1)} %convolution_convert_fusion), kind=kOutput, calls=%fused_computation.2 | convolution fusion | flops 4299161600 | bytes 12582912 | tf_op jit(solution)/shard_map/dot_general | solution.py:71
  36.0 0.0 reduce-scatter.4.cloned.1.call-update
  36.0 0.0 reduce-scatter.6.cloned.1.call-start
  36.1 98.0 %reduce-scatter.4.cloned.1.call-done = bf16[256,2048]{1,0:T(8,128)(2,1)} async-done(((bf16[2048,2048]{1,0:T(8,128)(2,1)}), bf16[256,2048]{1,0:T(8,128)(2,1)}) %reduce-scatter.4.cloned.1.call-update) | async-done | bytes 1048592 | tf_op jit(solution)/shard_map/reduce_scatter | solution.py:74
  134.0 0.0 reduce-scatter.6.cloned.1.call-update
  134.1 0.0 reduce-scatter.8.cloned.1.call-start
  134.1 0.1 copy.79
  134.2 0.1 convert_reduce_fusion.1
  134.4 0.1 select_reduce_fusion.3
  134.5 0.1 and_select_fusion.1
  134.6 0.1 copy.80
  134.7 0.1 eq.133
  134.8 0.1 eq.119
  135.0 0.2 convert_reduce_fusion
  135.1 0.1 fusion.26
  135.3 0.2 reduce_window_sum.11
  135.4 0.2 select_reduce_fusion
  135.6 0.1 reduce_sum.92
  135.8 0.1 copy.81
  135.8 0.1 select_reduce_fusion.2
  136.0 0.1 fusion.27
  136.0 23.9 %reduce-scatter.6.cloned.1.call-done = bf16[64,2048]{1,0:T(8,128)(2,1)} async-done(((bf16[256,2048]{1,0:T(8,128)(2,1)}), bf16[64,2048]{1,0:T(8,128)(2,1)}) %reduce-scatter.6.cloned.1.call-update) | async-done | bytes 262160 | tf_op jit(solution)/shard_map/reduce_scatter | solution.py:75
  160.0 1.1 fusion.15
  161.1 1.1 convolution_convert_fusion.1
  162.3 2.0 reshape.182
  164.3 21.4 %all_to_all.15 = bf16[1,32,4,2048]{3,2,0,1:T(4,128)(2,1)S(1)} all-to-all(bf16[1,32,4,2048]{3,2,0,1:T(4,128)(2,1)} %bitcast.84), channel_id=1, replica_groups=mesh['expert'=8,'tz'=8,'ty'=4] {'tz','ty'}, dimensions={1} | all-to-all | bytes 1048576 | tf_op jit(solution)/shard_map/all_to_all | solution.py:120
  185.7 0.3 copy.84
  186.0 0.5 tile.9
  186.5 57.6 %all_to_all.16 = bf16[8,1,32,4,2048]{4,2,3,1,0:T(8,128)(2,1)S(1)} all-to-all(bf16[8,1,32,4,2048]{4,2,3,1,0:T(8,128)(2,1)S(1)} %tile.9), channel_id=1, replica_groups=mesh['expert'=8,'tz'=8,'ty'=4] {'expert'}, dimensions={0} | all-to-all | bytes 8388608 | tf_op jit(solution)/shard_map/all_to_all | solution.py:123
  244.1 6.7 %fusion.6 = f32[8,1,32,4,2,704]{5,2,4,3,0,1:T(8,128)S(1)} fusion(bf16[1,2048,2,704]{1,3,2,0:T(8,128)(2,1)S(1)} %bitcast.87, bf16[8,1,32,4,2048]{4,2,3,1,0:T(8,128)(2,1)S(1)} %all_to_all.16), kind=kOutput, calls=%fused_computation.12 | convolution fusion | flops 5905580032 | bytes 15728640 | tf_op jit(solution)/shard_map/tsecd,sdgf->tsecgf/dot_general | solution.py:25
  250.8 1.0 fusion.4
  251.8 2.4 copy.85
  254.2 3.7 %convert_element_type.95 = bf16[1024,704]{1,0:T(8,128)(2,1)} reshape(bf16[8,1,32,4,1,704]{5,3,2,0,4,1:T(4,128)(2,1)} %copy.85) | data formatting | bytes 2883584 | tf_op jit(solution)/shard_map/convert_element_type | solution.py:28
  257.9 6.4 %convert_bitcast_fusion = bf16[1024,1,2048]{2,0,1:T(8,128)(2,1)} fusion(bf16[1024,704]{1,0:T(8,128)(2,1)} %convert_element_type.95, bf16[1,704,2048]{2,1,0:T(8,128)(2,1)S(1)} %copy-done), kind=kOutput, calls=%fused_computation.7 | convolution fusion | flops 2954887168 | bytes 8519680 | tf_op jit(solution)/shard_map/bsf,sfd->bsd/dot_general | solution.py:129
  264.3 0.0 reduce-scatter.8.cloned.1.call-update
  264.3 0.1 copy.90
  264.4 0.1 reshape.197
  264.6 0.1 copy.88
  264.7 0.1 mul.206
  264.8 0.1 copy.87
  264.9 0.1 mul.205
  265.1 34.3 %reduce-scatter.8.cloned.1.call-done = bf16[128,1,2048]{2,0,1:T(8,128)(2,1)} async-done(((bf16[1024,1,2048]{2,0,1:T(8,128)(2,1)}), bf16[128,1,2048]{2,0,1:T(8,128)(2,1)}) %reduce-scatter.8.cloned.1.call-update) | async-done | bytes 524304 | tf_op jit(solution)/shard_map/reduce_scatter | solution.py:128
  299.4 2.0 reshape.186
  301.5 9.7 %all-to-all-start.2 = ((bf16[32,4,1,2048]{3,1,2,0:T(4,128)(2,1)}), bf16[32,4,1,2048]{3,1,2,0:T(4,128)(2,1)}, u32[]{:S(2)}, u32[]{:S(2)}) async-start(bf16[32,4,1,2048]{3,1,2,0:T(4,128)(2,1)} %bitcast.83), calls=%async_computation.5 | async-start | bytes 1048576 | tf_op jit(solution)/shard_map/all_to_all | solution.py:137
  311.2 0.2 fusion.22
  311.5 1.0 gather_fusion.1
  312.5 0.1 reshape.200
  312.6 0.1 copy.91
  312.8 15.7 %all-to-all-done.2 = bf16[32,4,1,2048]{3,1,2,0:T(4,128)(2,1)} async-done(((bf16[32,4,1,2048]{3,1,2,0:T(4,128)(2,1)}), bf16[32,4,1,2048]{3,1,2,0:T(4,128)(2,1)}, u32[]{:S(2)}, u32[]{:S(2)}) %all-to-all-start.2) | async-done | bytes 524320 | tf_op jit(solution)/shard_map/all_to_all | solution.py:137
  328.5 1.2 reshape.187
  329.7 1.7 gather_fusion
  331.4 1.4 gather.11
  332.8 0.3 fusion.21
  333.1 1.2 multiply_reduce_fusion
  334.4 0.8 multiply_convert_fusion
  (44 shorter events, 0.2 us)
Async XLA Ops:
  7.2 250.8 %copy-start = (bf16[1,704,2048]{2,1,0:T(8,128)(2,1)S(1)}, bf16[1,704,2048]{2,1,0:T(8,128)(2,1)}, u32[]{:S(2)}) copy-start(bf16[1,704,2048]{2,1,0:T(8,128)(2,1)} %param.26) | copy-start | bytes 8650756
  7.2 5.7 %copy-start.5 = (f32[2048,2]{0,1:T(2,128)S(1)}, f32[2048,2]{0,1:T(2,128)}, u32[]{:S(2)}) copy-start(f32[2048,2]{0,1:T(2,128)} %param.17) | copy-start | bytes 49156
  7.2 6.1 %copy-start.4 = (s32[2048,2]{0,1:T(2,128)S(1)}, s32[2048,2]{0,1:T(2,128)}, u32[]{:S(2)}) copy-start(s32[2048,2]{0,1:T(2,128)} %param.16) | copy-start | bytes 49156
  7.2 126.8 %reduce-scatter.4.cloned.1.call-start = ((), (), s32[]{:S(2)}) async-start(), calls=%async_computation.6 | async-start | bytes 9437184 | tf_op jit(solution)/shard_map/reduce_scatter | solution.py:74
  14.7 14.3 %copy-start.11 = (bf16[8,64,2048]{2,1,0:T(8,128)(2,1)S(1)}, bf16[8,64,2048]{2,1,0:T(8,128)(2,1)}, u32[]{:S(2)}) copy-start(bf16[8,64,2048]{2,1,0:T(8,128)(2,1)} %param.18) | copy-start | bytes 6291460
  36.0 98.2 %copy-start.7 = (bf16[2048]{0:T(1024)(128)(2,1)S(1)}, bf16[2048]{0:T(1024)(128)(2,1)}, u32[]{:S(2)}) copy-start(bf16[2048]{0:T(1024)(128)(2,1)} %param.19) | copy-start | bytes 12292
  36.0 98.2 %copy-start.3 = (s32[64,2]{0,1:T(2,128)S(1)}, s32[64,2]{0,1:T(2,128)}, u32[]{:S(2)}) copy-start(s32[64,2]{0,1:T(2,128)} %param.21) | copy-start | bytes 1540
  36.0 98.3 %copy-start.6 = (s32[32]{0:T(128)S(1)}, s32[32]{0:T(128)}, u32[]{:S(2)}) copy-start(s32[32]{0:T(128)} %param.23) | copy-start | bytes 388
  36.0 98.5 %copy-start.9 = (s32[64,2]{0,1:T(2,128)S(1)}, s32[64,2]{0,1:T(2,128)}, u32[]{:S(2)}) copy-start(s32[64,2]{0,1:T(2,128)} %param.22) | copy-start | bytes 1540
  36.0 99.9 %copy-start.10 = (s32[32]{0:T(128)S(1)}, s32[32]{0:T(128)}, u32[]{:S(2)}) copy-start(s32[32]{0:T(128)} %param.24) | copy-start | bytes 388
  36.0 124.0 %copy-start.2 = (bf16[64,2048]{1,0:T(8,128)(2,1)S(1)}, bf16[64,2048]{1,0:T(8,128)(2,1)}, u32[]{:S(2)}) copy-start(bf16[64,2048]{1,0:T(8,128)(2,1)} %param.14) | copy-start | bytes 786436
  36.0 123.9 %reduce-scatter.6.cloned.1.call-start = ((), (), s32[]{:S(2)}) async-start(), calls=%async_computation.7 | async-start | bytes 1310720 | tf_op jit(solution)/shard_map/reduce_scatter | solution.py:75
  134.1 165.4 %reduce-scatter.8.cloned.1.call-start = ((), (), s32[]{:S(2)}) async-start(), calls=%async_computation.8 | async-start | bytes 4718592 | tf_op jit(solution)/shard_map/reduce_scatter | solution.py:128
  161.1 150.1 %copy-start.1 = (bf16[64,2048]{1,0:T(8,128)(2,1)}, bf16[64,2048]{1,0:T(8,128)(2,1)S(1)}, u32[]{:S(2)}) copy-start(bf16[64,2048]{1,0:T(8,128)(2,1)S(1)} %get-tuple-element.9) | copy-start | bytes 786436
  186.0 58.1 %slice-start = ((s8[5767168]{0:T(1024)(128)(4,1)}), s8[4194304]{0:T(1024)(128)(4,1)S(1)}, s32[]{:S(2)}) async-start(s8[5767168]{0:T(1024)(128)(4,1)} %bitcast.86), calls=%async_computation.9 | async-start | bytes 8388608
  186.5 57.6 %slice-start.1 = ((s8[5767168]{0:T(1024)(128)(4,1)}), s8[1572864]{0:T(1024)(128)(4,1)S(1)}, s32[]{:S(2)}) async-start(s8[5767168]{0:T(1024)(128)(4,1)} %bitcast.86), calls=%async_computation.10 | async-start | bytes 3145728
  264.3 0.8 copy-start.8
  264.3 46.9 %copy-start.12 = (bf16[2048,8]{0,1:T(8,128)(2,1)S(1)}, bf16[2048,8]{0,1:T(8,128)(2,1)}, u32[]{:S(2)}) copy-start(bf16[2048,8]{0,1:T(8,128)(2,1)} %param.20) | copy-start | bytes 98308
  301.5 27.0 %all-to-all-start.2 = ((bf16[32,4,1,2048]{3,1,2,0:T(4,128)(2,1)}), bf16[32,4,1,2048]{3,1,2,0:T(4,128)(2,1)}, u32[]{:S(2)}, u32[]{:S(2)}) async-start(bf16[32,4,1,2048]{3,1,2,0:T(4,128)(2,1)} %bitcast.83), calls=%async_computation.5 | async-start | bytes 1048576 | tf_op jit(solution)/shard_map/all_to_all | solution.py:137
Sparse Core Ops, SparseCore 0:
  36.1 97.8 reduce-scatter.3
  136.6 23.3 reduce-scatter.5
  264.4 34.9 reduce-scatter.7
